TPU v7x, 32 devices: a whole 2x2x4 slice. The times are simulated.
32 devices in a mesh: row: 8 (over y, x, core), col: 4 (over z).
Axes of the slice: x: 2, y: 2, z: 4, core: 2. Of those that a mesh axis runs over, the one named last changes fastest.
Arguments:
- pair: bfloat16 [256, 256, 128], P('row', 'col'), may hold values from -6 to 6
- mask: int32 [256], replicated, may hold values 0 or 1
- w_agate: bfloat16 [128, 128], replicated, may hold values from -0.5 to 0.5
- w_aproj: bfloat16 [128, 128], replicated, may hold values from -0.5 to 0.5
- w_bgate: bfloat16 [128, 128], replicated, may hold values from -0.5 to 0.5
- w_bproj: bfloat16 [128, 128], replicated, may hold values from -0.5 to 0.5
- w_gate: bfloat16 [128, 128], replicated, may hold values from -0.5 to 0.5
- w_out: bfloat16 [128, 128], replicated, may hold values from -0.5 to 0.5
- w_up: bfloat16 [128, 512], replicated, may hold values from -0.5 to 0.5
- w_down: bfloat16 [512, 128], replicated, may hold values from -0.25 to 0.25
Outputs:
- updated: bfloat16 [256, 256, 128], P('row', 'col')
All inputs are finite; a program needn't handle non-finite values.
Results may differ from a plain program's by a relative error of at most 0.0059.
Values may be sent and summed in bfloat16 or wider, within the bound.
No kernel may reach another device: no remote copies, remote signals or barrier semaphores. Data moves between devices by JAX's collectives and lax.ppermute only.
A program may use at most 64 MiB of HBM per device.

v0:
```python
import jax
import jax.numpy as jnp
from jax import lax
from jax.sharding import PartitionSpec as P


def layer_norm(values):
    center = values - jnp.mean(values, axis=-1, keepdims=True)
    spread = jnp.mean(center * center, axis=-1, keepdims=True)
    return center * lax.rsqrt(spread + 1e-05)


def body(pair, mask, w_agate, w_aproj, w_bgate, w_bproj, w_gate, w_out, w_up, w_down):
    rows, cols, width = pair.shape
    present = mask.astype(jnp.float32)
    row_start = lax.axis_index("row") * rows
    col_start = lax.axis_index("col") * cols
    row_mask = lax.dynamic_slice_in_dim(present, row_start, rows, 0)
    col_mask = lax.dynamic_slice_in_dim(present, col_start, cols, 0)
    pair_mask = (row_mask[:, None] * col_mask[None, :]).reshape(rows * cols, 1)
    pair_flat = pair.astype(jnp.float32).reshape(rows * cols, width)
    normed = layer_norm(pair_flat).astype(jnp.bfloat16)
    gate = jax.nn.sigmoid(jnp.dot(normed, w_gate, preferred_element_type=jnp.float32))
    left = (
        jax.nn.sigmoid(jnp.dot(normed, w_agate, preferred_element_type=jnp.float32))
        * jnp.dot(normed, w_aproj, preferred_element_type=jnp.float32)
        * pair_mask
    )
    right = (
        jax.nn.sigmoid(jnp.dot(normed, w_bgate, preferred_element_type=jnp.float32))
        * jnp.dot(normed, w_bproj, preferred_element_type=jnp.float32)
        * pair_mask
    )
    left_major = jnp.transpose(left.astype(jnp.bfloat16).reshape(rows, cols, -1), (2, 0, 1))
    right_major = jnp.transpose(right.astype(jnp.bfloat16).reshape(rows, cols, -1), (2, 0, 1))
    left_spread, right_spread = (
        lax.all_to_all(
            lax.all_to_all(left_major, "row", split_axis=0, concat_axis=1, tiled=True),
            "col",
            split_axis=1,
            concat_axis=2,
            tiled=True,
        ),
        lax.all_to_all(
            lax.all_to_all(right_major, "row", split_axis=0, concat_axis=1, tiled=True),
            "col",
            split_axis=1,
            concat_axis=2,
            tiled=True,
        ),
    )
    mixed = jnp.einsum(
        "cik,cjk->cij",
        lax.all_gather(left_spread, "col", axis=1, tiled=True),
        right_spread,
        preferred_element_type=jnp.float32,
    ).astype(jnp.bfloat16)
    mixed = lax.all_to_all(mixed, "row", split_axis=1, concat_axis=0, tiled=True)
    mixed_rows = jnp.transpose(mixed, (1, 2, 0)).astype(jnp.float32).reshape(rows * cols, -1)
    mixed_normed = layer_norm(mixed_rows).astype(jnp.bfloat16)
    middle = pair_flat + gate * jnp.dot(mixed_normed, w_out, preferred_element_type=jnp.float32)
    trans_in = layer_norm(middle).astype(jnp.bfloat16)
    trans_hidden = jax.nn.relu(jnp.dot(trans_in, w_up, preferred_element_type=jnp.float32)).astype(
        jnp.bfloat16
    )
    result = middle + jnp.dot(trans_hidden, w_down, preferred_element_type=jnp.float32)
    return result.astype(jnp.bfloat16).reshape(rows, cols, width)


def solution(mesh):
    placed = (P("row", "col", None), P(), P(), P(), P(), P(), P(), P(), P(), P())
    return jax.shard_map(
        body, mesh=mesh, in_specs=placed, out_specs=P("row", "col", None), check_vma=False
    )
```

profile of v0, /device:TPU:0, one launch (start us, length us, event | category | flops | bytes accessed | tf_op | source)
XLA Modules:
  0.0 144.5 jit_solution(13755586689063979857)
XLA Ops:
  6.5 1.4 convert_reduce_fusion
  8.0 1.7 %multiply_reduce_fusion.2 = f32[32,64]{1,0:T(8,128)S(1)} fusion(bf16[32,64,128]{2,1,0:T(8,128)(2,1)} %param.10, f32[32,64]{1,0:T(8,128)S(1)} %broadcast_multiply_fusion.2), kind=kLoop, calls=%fused_computation.36 | loop fusion | flops 1046528 | bytes 540672 | tf_op jit(solution)/shard_map/reduce_sum | solution.py:9
  9.7 0.1 div.32
  9.7 0.7 convert_element_type.47
  10.4 0.1 dynamic_slice.6
  10.5 0.1 dynamic_slice.7
  10.6 0.1 broadcast_multiply_fusion
  10.7 0.1 mul.93
  10.7 0.1 rsqrt.31
  10.8 1.6 %fusion.18 = bf16[2048,128]{1,0:T(8,128)(2,1)S(1)} fusion(bf16[32,64,128]{2,1,0:T(8,128)(2,1)} %param.10, f32[2048]{0:T(1024)S(1)} %rsqrt.31, f32[2048]{0:T(1024)S(1)} %div.32), kind=kLoop, calls=%fused_computation.33 | loop fusion | flops 1048576 | bytes 1064960 | tf_op jit(solution)/shard_map/convert_element_type | solution.py:22
  12.5 0.0 copy-start.3
  12.5 0.4 fusion.8
  12.9 0.3 copy-done.3
  13.2 0.4 fusion.12
  13.6 1.6 %copy.22 = bf16[32,64,128]{1,0,2:T(8,128)(2,1)S(1)} copy(bf16[32,64,128]{2,1,0:T(8,128)(2,1)S(1)} %bitcast.89) | data formatting | bytes 1048576 | tf_op jit(solution)/shard_map/reshape | solution.py:34
  15.2 0.7 reshape.119
  15.9 14.7 %all_to_all.81 = bf16[8,2,16384]{2,1,0:T(2,128)(2,1)S(1)} all-to-all(bf16[8,2,16384]{2,1,0:T(2,128)(2,1)S(1)} %reshape.119), channel_id=1, replica_groups=mesh['row'=8,'col'=4] {'row'}, dimensions={0} | all-to-all | bytes 1048576 | tf_op jit(solution)/shard_map/all_to_all | solution.py:38
  30.7 0.7 reshape.120
  31.3 0.1 copy.23
  31.4 0.7 copy.47
  32.1 0.9 reshape.121
  33.0 18.5 %all_to_all.82 = bf16[4,2,32768]{2,1,0:T(2,128)(2,1)S(1)} all-to-all(bf16[4,2,32768]{2,1,0:T(2,128)(2,1)S(1)} %reshape.121), channel_id=1, replica_groups=mesh['row'=8,'col'=4] {'col'}, dimensions={0} | all-to-all | bytes 1048576 | tf_op jit(solution)/shard_map/all_to_all | solution.py:37
  51.5 0.7 reshape.122
  52.2 0.0 copy-start.8
  52.2 0.8 copy.45
  53.0 1.5 %all_to_all.66 = bf16[16,64,256]{2,1,0:T(8,128)(2,1)} reshape(bf16[16,64,4,64]{3,2,1,0:T(4,128)(2,1)S(1)} %bitcast.81) | data formatting | bytes 1048576 | tf_op jit(solution)/shard_map/all_to_all | solution.py:37
  54.5 0.0 all-gather.2.cloned.1.call-update
  54.5 0.0 copy-start.4
  54.6 0.4 fusion.4
  55.0 0.3 copy-done.4
  55.3 0.4 fusion.13
  55.7 1.6 %copy.27 = bf16[32,64,128]{1,0,2:T(8,128)(2,1)S(1)} copy(bf16[32,64,128]{2,1,0:T(8,128)(2,1)S(1)} %bitcast.88) | data formatting | bytes 1048576 | tf_op jit(solution)/shard_map/reshape | solution.py:35
  57.3 0.7 reshape.123
  58.0 12.2 %all_to_all.83 = bf16[8,2,16384]{2,1,0:T(2,128)(2,1)S(1)} all-to-all(bf16[8,2,16384]{2,1,0:T(2,128)(2,1)S(1)} %reshape.123), channel_id=1, replica_groups=mesh['row'=8,'col'=4] {'row'}, dimensions={0} | all-to-all | bytes 1048576 | tf_op jit(solution)/shard_map/all_to_all | solution.py:45
  70.2 0.7 reshape.124
  70.8 0.1 copy.28
  70.9 0.7 copy.46
  71.6 0.9 reshape.125
  72.5 31.4 %all_to_all.84 = bf16[4,2,32768]{2,1,0:T(2,128)(2,1)S(1)} all-to-all(bf16[4,2,32768]{2,1,0:T(2,128)(2,1)S(1)} %reshape.125), channel_id=1, replica_groups=mesh['row'=8,'col'=4] {'col'}, dimensions={0} | all-to-all | bytes 1048576 | tf_op jit(solution)/shard_map/all_to_all | solution.py:44
  103.9 0.7 reshape.126
  104.6 0.8 copy.44
  105.4 0.7 all_to_all.74
  106.1 3.6 %all-gather.2.cloned.1.call-done = bf16[16,256,256]{2,1,0:T(8,128)(2,1)} async-done(((bf16[16,64,256]{2,1,0:T(8,128)(2,1)}), bf16[16,256,256]{2,1,0:T(8,128)(2,1)}) %all-gather.2.cloned.1.call-update) | async-done | bytes 2097168 | tf_op jit(solution)/shard_map/all_gather | solution.py:54
  109.7 2.3 %convolution_convert_fusion = bf16[16,256,64]{1,2,0:T(8,128)(2,1)S(1)} fusion(bf16[16,256,256]{2,1,0:T(8,128)(2,1)} %all-gather.2.cloned.1.call-done, bf16[16,64,256]{2,1,0:T(8,128)(2,1)S(1)} %all_to_all.74), kind=kOutput, calls=%fused_computation.25 | convolution fusion | flops 134479872 | bytes 3145728 | tf_op jit(solution)/shard_map/cik,cjk->cij/dot_general | solution.py:52
  112.0 0.0 copy-start.9
  112.0 1.0 copy.32
  113.0 1.5 %reshape.127 = bf16[8,2,16384]{2,1,0:T(2,128)(2,1)} reshape(bf16[256,16,64]{2,1,0:T(8,128)(2,1)S(1)} %bitcast.76) | data formatting | bytes 1048576
  114.5 3.7 %all-to-all-start.4 = ((bf16[8,2,16384]{2,1,0:T(2,128)(2,1)}), bf16[8,2,16384]{2,1,0:T(2,128)(2,1)S(1)}, u32[]{:S(2)}, u32[]{:S(2)}) async-start(bf16[8,2,16384]{2,1,0:T(2,128)(2,1)} %reshape.127), calls=%async_computation.4 | async-start | bytes 1048576 | tf_op jit(solution)/shard_map/all_to_all | solution.py:58
  118.2 1.4 fusion.11
  119.6 8.3 %all-to-all-done.4 = bf16[8,2,16384]{2,1,0:T(2,128)(2,1)S(1)} async-done(((bf16[8,2,16384]{2,1,0:T(2,128)(2,1)}), bf16[8,2,16384]{2,1,0:T(2,128)(2,1)S(1)}, u32[]{:S(2)}, u32[]{:S(2)}) %all-to-all-start.4) | async-done | bytes 524320 | tf_op jit(solution)/shard_map/all_to_all | solution.py:58
  127.9 0.7 reshape.128
  128.6 0.3 copy.33
  128.8 0.3 convert_bitcast_fusion
  129.1 0.2 copy.34
  129.4 0.2 bitcast_reduce_fusion
  129.6 0.3 multiply_reduce_fusion
  129.9 0.1 div.38
  130.0 0.1 rsqrt.33
  130.1 2.3 %copy.35 = f32[32,64,128]{2,1,0:T(8,128)} copy(f32[32,64,128]{1,0,2:T(8,128)S(1)} %bitcast.71) | data formatting | bytes 2097152 | tf_op jit(solution)/shard_map/convert_element_type | solution.py:59
  132.4 1.9 %fusion.16 = bf16[2048,128]{1,0:T(8,128)(2,1)S(1)} fusion(f32[32,64,128]{2,1,0:T(8,128)} %copy.35, f32[2048]{0:T(1024)S(1)} %rsqrt.33, f32[2048]{0:T(1024)S(1)} %div.38), kind=kLoop, calls=%fused_computation.28 | loop fusion | flops 786432 | bytes 1589248 | tf_op jit(solution)/shard_map/convert_element_type | solution.py:60
  134.3 0.0 copy-start.6
  134.4 0.5 fusion.24
  134.9 0.6 multiply_reduce_fusion.1
  135.5 2.1 %fusion.14 = bf16[2048,128]{1,0:T(8,128)(2,1)} fusion(f32[2048,128]{1,0:T(8,128)S(1)} %get-tuple-element.6, bf16[512,128]{1,0:T(8,128)(2,1)S(1)} %copy-done, bf16[128,512]{1,0:T(8,128)(2,1)S(1)} %copy-done.6, f32[2048]{0:T(1024)S(1)} %add_rsqrt_fusion.2, f32[2048]{0:T(1024)S(1)} %broadcast_multiply_fusion.3), kind=kOutput, calls=%fused_computation.22 | convolution fusion | flops 540278784 | bytes 1851392 | tf_op jit(solution)/shard_map/dot_general | solution.py:66
  (20 shorter events, 0.1 us)
Async XLA Ops:
  6.5 129.0 %copy-start = (bf16[512,128]{1,0:T(8,128)(2,1)S(1)}, bf16[512,128]{1,0:T(8,128)(2,1)}, u32[]{:S(2)}) copy-start(bf16[512,128]{1,0:T(8,128)(2,1)} %param.19) | copy-start | bytes 393220
  6.5 5.9 %copy-start.7 = (bf16[128,128]{1,0:T(8,128)(2,1)S(1)}, bf16[128,128]{1,0:T(8,128)(2,1)}, u32[]{:S(2)}) copy-start(bf16[128,128]{1,0:T(8,128)(2,1)} %param.12) | copy-start | bytes 98308
  6.5 103.1 %all-gather.2.cloned.1.call-start = ((), (), s32[]{:S(2)}) async-start(), calls=%async_computation.5 | async-start | bytes 2621440 | tf_op jit(solution)/shard_map/all_gather | solution.py:54
  12.5 0.8 copy-start.3
  52.2 2.3 %copy-start.8 = (bf16[128,128]{1,0:T(8,128)(2,1)S(1)}, bf16[128,128]{1,0:T(8,128)(2,1)}, u32[]{:S(2)}) copy-start(bf16[128,128]{1,0:T(8,128)(2,1)} %param.14) | copy-start | bytes 98308
  54.5 0.8 copy-start.4
  112.0 6.2 %copy-start.9 = (bf16[128,128]{1,0:T(8,128)(2,1)S(1)}, bf16[128,128]{1,0:T(8,128)(2,1)}, u32[]{:S(2)}) copy-start(bf16[128,128]{1,0:T(8,128)(2,1)} %param.16) | copy-start | bytes 98308
  114.5 13.4 %all-to-all-start.4 = ((bf16[8,2,16384]{2,1,0:T(2,128)(2,1)}), bf16[8,2,16384]{2,1,0:T(2,128)(2,1)S(1)}, u32[]{:S(2)}, u32[]{:S(2)}) async-start(bf16[8,2,16384]{2,1,0:T(2,128)(2,1)} %reshape.127), calls=%async_computation.4 | async-start | bytes 1048576 | tf_op jit(solution)/shard_map/all_to_all | solution.py:58
  130.0 4.3 %copy-start.1 = (bf16[32,64,128]{2,1,0:T(8,128)(2,1)S(1)}, bf16[32,64,128]{2,1,0:T(8,128)(2,1)}, u32[]{:S(2)}) copy-start(bf16[32,64,128]{2,1,0:T(8,128)(2,1)} %param.10) | copy-start | bytes 1572868
  130.1 4.3 %copy-start.5 = (bf16[128,128]{1,0:T(8,128)(2,1)S(1)}, bf16[128,128]{1,0:T(8,128)(2,1)}, u32[]{:S(2)}) copy-start(bf16[128,128]{1,0:T(8,128)(2,1)} %param.17) | copy-start | bytes 98308
  132.4 1.9 %copy-start.2 = (f32[2048,128]{1,0:T(8,128)S(1)}, f32[2048,128]{1,0:T(8,128)}, u32[]{:S(2)}) copy-start(f32[2048,128]{1,0:T(8,128)} %fusion.11) | copy-start | bytes 3145732
  134.3 1.2 copy-start.6
Sparse Core Ops, SparseCore 0:
  54.6 54.9 all-gather.1
where the time goes:
time: 145 us
  blocking collectives  76.8 us (53%)
  local copies, waits for them, and re-layouts  21.5 us (15%)
  between operations  13.7 us (9%)
  waiting for transfers between devices  11.9 us (8%)
  other arithmetic  8.91 us (6%)
  matrix products  7.95 us (5%)
  starting transfers between devices  3.69 us (3%)
    all_to_all x1, blocking collectives, body(): lax.all_to_all(lax.all_to_all(right_major, 'row', split_axis=0, concat_ax...  31.4 us
    all_to_all x1, blocking collectives, body(): lax.all_to_all(lax.all_to_all(left_major, 'row', split_axis=0, concat_axi...  18.5 us
    all_to_all x1, blocking collectives, body(): lax.all_to_all(left_major, 'row', split_axis=0, concat_axis=1, tiled=True)  14.7 us
    all_to_all x1, blocking collectives, body(): lax.all_to_all(right_major, 'row', split_axis=0, concat_axis=1, tiled=True)  12.2 us
    unnamed x30, local copies, waits for them, and re-layouts  8.68 us
    all_to_all x1, waiting for transfers between devices, body(): lax.all_to_all(mixed, 'row', split_axis=1, concat_axis=0, tiled=True)  8.32 us
    all_to_all x1, starting transfers between devices, body(): lax.all_to_all(mixed, 'row', split_axis=1, concat_axis=0, tiled=True)  3.69 us
    all_gather x1, waiting for transfers between devices, body(): lax.all_gather(left_spread, 'col', axis=1, tiled=True)  3.59 us
  transfers between devices with their start and end apart: 2, of which 2 were waited for; matrix products, arithmetic and copies ran while one was open for 6% of the time, Pallas kernels for 0%

commit v1 on v0

--- a/solution.py
+++ b/solution.py
@@ -2,6 +2,24 @@
 import jax.numpy as jnp
 from jax import lax
 from jax.sharding import PartitionSpec as P
+
+
+def ring_gather(array, axis, dim):
+    ways, here, step = (lax.axis_size(axis), lax.axis_index(axis), array.shape[dim])
+    shape = [n * ways if d == dim else n for d, n in enumerate(array.shape)]
+    full = lax.dynamic_update_slice_in_dim(
+        jnp.zeros(shape, array.dtype), array, here * step, axis=dim
+    )
+    going_up = going_down = array
+    for far in range(1, ways // 2 + 1):
+        going_up = lax.ppermute(going_up, axis, [(d, (d + 1) % ways) for d in range(ways)])
+        full = lax.dynamic_update_slice_in_dim(full, going_up, (here - far) % ways * step, axis=dim)
+        if 2 * far < ways:
+            going_down = lax.ppermute(going_down, axis, [(d, (d - 1) % ways) for d in range(ways)])
+            full = lax.dynamic_update_slice_in_dim(
+                full, going_down, (here + far) % ways * step, axis=dim
+            )
+    return full
 
 
 def layer_norm(values):
@@ -51,7 +69,7 @@
     )
     mixed = jnp.einsum(
         "cik,cjk->cij",
-        lax.all_gather(left_spread, "col", axis=1, tiled=True),
+        ring_gather(left_spread, "col", 1),
         right_spread,
         preferred_element_type=jnp.float32,
     ).astype(jnp.bfloat16)

time: 145 us -> 134 us (0.924)
  blocking collectives: 76.8 us -> 0 us
  waiting for transfers between devices: 11.9 us -> 53.2 us
  starting transfers between devices: 3.69 us -> 35.2 us
  between operations: 13.7 us -> 0.39 us
  local copies, waits for them, and re-layouts: 21.5 us -> 29.1 us
  matrix products: 7.95 us -> 6.33 us
    all_to_all x4 -> x0, blocking collectives: 76.8 us -> none  [the longest x1 31.4 us: body(): lax.all_to_all(lax.all_to_all(right_major, 'row', split_axis=0, concat_ax...]
    ppermute x0 -> x3, waiting for transfers between devices: none -> 23.6 us  [the longest x2 23.6 us: ring_gather(): lax.ppermute(going_up, axis, [(d, (d + 1) % ways) for d in range(ways)])]
    all_to_all x0 -> x4, waiting for transfers between devices: none -> 21.3 us  [the longest x1 9.13 us: body(): lax.all_to_all(lax.all_to_all(left_major, 'row', split_axis=0, concat_axi...]
    all_to_all x0 -> x4, starting transfers between devices: none -> 17.2 us  [the longest x1 5.17 us: body(): lax.all_to_all(left_major, 'row', split_axis=0, concat_axis=1, tiled=True)]
    ppermute x0 -> x3, starting transfers between devices: none -> 11.9 us  [the longest x2 9.84 us: ring_gather(): lax.ppermute(going_up, axis, [(d, (d + 1) % ways) for d in range(ways)])]
    dynamic_update_slice x0 -> x4, local copies, waits for them, and re-layouts: none -> 4.33 us  [the longest x2 2.16 us: ring_gather(): lax.dynamic_update_slice_in_dim(full, going_up, (here - far) % ways * ste...]
    all_gather x1 -> x0, waiting for transfers between devices: 3.59 us -> none  [body(): lax.all_gather(left_spread, 'col', axis=1, tiled=True)]
    unnamed x30, local copies, waits for them, and re-layouts: 8.68 us -> 11.7 us
  transfers between devices with their start and end apart: 2 -> 8, of which waited for: 2 -> 6; matrix products, arithmetic and copies ran while one was open for 6% -> 13% of each run, Pallas kernels for 0% -> 0%
where the time goes in v1:
time: 134 us; the launch traced here: 133 us
  waiting for transfers between devices  53.2 us (40%)
  starting transfers between devices  35.2 us (26%)
  local copies, waits for them, and re-layouts  29.1 us (22%)
  other arithmetic  8.91 us (7%)
  matrix products  6.33 us (5%)
    ppermute x2, waiting for transfers between devices, ring_gather(): lax.ppermute(going_up, axis, [(d, (d + 1) % ways) for d in range(ways)])  23.6 us
    unnamed x30, local copies, waits for them, and re-layouts  11.7 us
    ppermute x2, starting transfers between devices, ring_gather(): lax.ppermute(going_up, axis, [(d, (d + 1) % ways) for d in range(ways)])  9.84 us
    all_to_all x1, waiting for transfers between devices, body(): lax.all_to_all(lax.all_to_all(left_major, 'row', split_axis=0, concat_axi...  9.13 us
    all_to_all x1, waiting for transfers between devices, body(): lax.all_to_all(mixed, 'row', split_axis=1, concat_axis=0, tiled=True)  8.35 us
    all_to_all x1, waiting for transfers between devices, body(): lax.all_to_all(right_major, 'row', split_axis=0, concat_axis=1, tiled=True)  6.66 us
    all_to_all x1, starting transfers between devices, body(): lax.all_to_all(mixed, 'row', split_axis=1, concat_axis=0, tiled=True)  6.11 us
    all_to_all x1, waiting for transfers between devices, body(): lax.all_to_all(left_major, 'row', split_axis=0, concat_axis=1, tiled=True)  5.48 us
  transfers between devices with their start and end apart: 8, of which 6 were waited for; matrix products, arithmetic and copies ran while one was open for 13% of the time, Pallas kernels for 0%

profile of v1, /device:TPU:0, one launch (start us, length us, event | category | flops | bytes accessed | tf_op | source)
XLA Modules:
  0.0 133.1 jit_solution(7841551384834888184)
XLA Ops:
  0.0 1.4 %convert_reduce_fusion = f32[32,64]{1,0:T(8,128)S(1)} fusion(bf16[32,64,128]{2,1,0:T(8,128)(2,1)} %param.10), kind=kLoop, calls=%fused_computation.37 | loop fusion | flops 522240 | bytes 532480 | tf_op jit(solution)/shard_map/reduce_sum | solution.py:26
  1.4 1.7 %multiply_reduce_fusion.2 = f32[32,64]{1,0:T(8,128)S(1)} fusion(bf16[32,64,128]{2,1,0:T(8,128)(2,1)} %param.10, f32[32,64]{1,0:T(8,128)S(1)} %broadcast_multiply_fusion.2), kind=kLoop, calls=%fused_computation.36 | loop fusion | flops 1046528 | bytes 540672 | tf_op jit(solution)/shard_map/reduce_sum | solution.py:27
  3.2 0.7 convert_element_type.47
  3.9 0.1 dynamic_slice.7
  4.0 0.1 broadcast_multiply_fusion
  4.3 1.6 %fusion.18 = bf16[2048,128]{1,0:T(8,128)(2,1)S(1)} fusion(bf16[32,64,128]{2,1,0:T(8,128)(2,1)} %param.10, f32[2048]{0:T(1024)S(1)} %rsqrt.31, f32[2048]{0:T(1024)S(1)} %div.32), kind=kLoop, calls=%fused_computation.33 | loop fusion | flops 1048576 | bytes 1064960 | tf_op jit(solution)/shard_map/convert_element_type | solution.py:40
  5.9 0.4 fusion.8
  6.4 0.3 copy-done.3
  6.7 0.4 fusion.12
  7.1 1.6 %copy.32 = bf16[32,64,128]{1,0,2:T(8,128)(2,1)S(1)} copy(bf16[32,64,128]{2,1,0:T(8,128)(2,1)S(1)} %bitcast.89) | data formatting | bytes 1048576 | tf_op jit(solution)/shard_map/reshape | solution.py:52
  8.7 1.5 %reshape.119 = bf16[8,2,16384]{2,1,0:T(2,128)(2,1)} reshape(bf16[128,32,64]{2,1,0:T(8,128)(2,1)S(1)} %bitcast.74) | data formatting | bytes 1048576
  10.2 5.2 %all-to-all-start = ((bf16[8,2,16384]{2,1,0:T(2,128)(2,1)}), bf16[8,2,16384]{2,1,0:T(2,128)(2,1)S(1)}, u32[]{:S(2)}, u32[]{:S(2)}) async-start(bf16[8,2,16384]{2,1,0:T(2,128)(2,1)} %reshape.119), calls=%async_computation | async-start | bytes 1048576 | tf_op jit(solution)/shard_map/all_to_all | solution.py:56
  15.4 0.4 fusion.4
  15.8 0.3 copy-done.4
  16.1 0.4 fusion.13
  16.5 1.6 %copy.37 = bf16[32,64,128]{1,0,2:T(8,128)(2,1)S(1)} copy(bf16[32,64,128]{2,1,0:T(8,128)(2,1)S(1)} %bitcast.88) | data formatting | bytes 1048576 | tf_op jit(solution)/shard_map/reshape | solution.py:53
  18.1 1.5 %reshape.123 = bf16[8,2,16384]{2,1,0:T(2,128)(2,1)} reshape(bf16[128,32,64]{2,1,0:T(8,128)(2,1)S(1)} %bitcast.75) | data formatting | bytes 1048576
  19.6 5.5 %all-to-all-done = bf16[8,2,16384]{2,1,0:T(2,128)(2,1)S(1)} async-done(((bf16[8,2,16384]{2,1,0:T(2,128)(2,1)}), bf16[8,2,16384]{2,1,0:T(2,128)(2,1)S(1)}, u32[]{:S(2)}, u32[]{:S(2)}) %all-to-all-start) | async-done | bytes 524320 | tf_op jit(solution)/shard_map/all_to_all | solution.py:56
  25.1 3.5 %all-to-all-start.2 = ((bf16[8,2,16384]{2,1,0:T(2,128)(2,1)}), bf16[8,2,16384]{2,1,0:T(2,128)(2,1)S(1)}, u32[]{:S(2)}, u32[]{:S(2)}) async-start(bf16[8,2,16384]{2,1,0:T(2,128)(2,1)} %reshape.123), calls=%async_computation.2 | async-start | bytes 1048576 | tf_op jit(solution)/shard_map/all_to_all | solution.py:63
  28.6 0.7 reshape.120
  29.3 0.1 copy.33
  29.4 0.7 copy.57
  30.1 1.6 %reshape.121 = bf16[4,2,32768]{2,1,0:T(2,128)(2,1)} reshape(bf16[256,16,64]{2,1,0:T(8,128)(2,1)S(1)} %bitcast.79) | data formatting | bytes 1048576
  31.6 6.7 %all-to-all-done.2 = bf16[8,2,16384]{2,1,0:T(2,128)(2,1)S(1)} async-done(((bf16[8,2,16384]{2,1,0:T(2,128)(2,1)}), bf16[8,2,16384]{2,1,0:T(2,128)(2,1)S(1)}, u32[]{:S(2)}, u32[]{:S(2)}) %all-to-all-start.2) | async-done | bytes 524320 | tf_op jit(solution)/shard_map/all_to_all | solution.py:63
  38.3 4.9 %all-to-all-start.1 = ((bf16[4,2,32768]{2,1,0:T(2,128)(2,1)}), bf16[4,2,32768]{2,1,0:T(2,128)(2,1)S(1)}, u32[]{:S(2)}, u32[]{:S(2)}) async-start(bf16[4,2,32768]{2,1,0:T(2,128)(2,1)} %reshape.121), calls=%async_computation.1 | async-start | bytes 1048576 | tf_op jit(solution)/shard_map/all_to_all | solution.py:55
  43.2 0.7 reshape.124
  43.8 0.1 copy.38
  44.0 0.7 copy.56
  44.6 1.5 %reshape.125 = bf16[4,2,32768]{2,1,0:T(2,128)(2,1)} reshape(bf16[256,16,64]{2,1,0:T(8,128)(2,1)S(1)} %bitcast.82) | data formatting | bytes 1048576
  46.2 9.1 %all-to-all-done.1 = bf16[4,2,32768]{2,1,0:T(2,128)(2,1)S(1)} async-done(((bf16[4,2,32768]{2,1,0:T(2,128)(2,1)}), bf16[4,2,32768]{2,1,0:T(2,128)(2,1)S(1)}, u32[]{:S(2)}, u32[]{:S(2)}) %all-to-all-start.1) | async-done | bytes 524320 | tf_op jit(solution)/shard_map/all_to_all | solution.py:55
  55.3 3.6 %all-to-all-start.3 = ((bf16[4,2,32768]{2,1,0:T(2,128)(2,1)}), bf16[4,2,32768]{2,1,0:T(2,128)(2,1)S(1)}, u32[]{:S(2)}, u32[]{:S(2)}) async-start(bf16[4,2,32768]{2,1,0:T(2,128)(2,1)} %reshape.125), calls=%async_computation.3 | async-start | bytes 1048576 | tf_op jit(solution)/shard_map/all_to_all | solution.py:62
  59.0 0.7 reshape.122
  59.7 0.8 copy.55
  60.5 1.5 %all_to_all.66 = bf16[16,64,256]{2,1,0:T(8,128)(2,1)} reshape(bf16[16,64,4,64]{3,2,1,0:T(4,128)(2,1)S(1)} %bitcast.84) | data formatting | bytes 1048576 | tf_op jit(solution)/shard_map/all_to_all | solution.py:55
  62.0 1.8 %collective-permute-start = (bf16[16,64,256]{2,1,0:T(8,128)(2,1)}, bf16[16,64,256]{2,1,0:T(8,128)(2,1)}, u32[]{:S(2)}, u32[]{:S(2)}) collective-permute-start(bf16[16,64,256]{2,1,0:T(8,128)(2,1)} %all_to_all.66), channel_id=1, source_target_pairs={{0,1},{1,2},{2,3},{3,0},{4,5},{5,6},{6,7},{7,4},{8,9},{9,10},{10,1... | collective-permute-start | bytes 1572872 | tf_op jit(solution)/shard_map/ppermute | solution.py:15
  63.8 2.0 %collective-permute-start.1 = (bf16[16,64,256]{2,1,0:T(8,128)(2,1)}, bf16[16,64,256]{2,1,0:T(8,128)(2,1)}, u32[]{:S(2)}, u32[]{:S(2)}) collective-permute-start(bf16[16,64,256]{2,1,0:T(8,128)(2,1)} %all_to_all.66), channel_id=1, source_target_pairs={{0,3},{1,0},{2,1},{3,2},{4,7},{5,4},{6,5},{7,6},{8,11},{9,8},{10,9... | collective-permute-start | bytes 1572872 | tf_op jit(solution)/shard_map/ppermute | solution.py:18
  65.8 18.4 %collective-permute-done = bf16[16,64,256]{2,1,0:T(8,128)(2,1)} collective-permute-done((bf16[16,64,256]{2,1,0:T(8,128)(2,1)}, bf16[16,64,256]{2,1,0:T(8,128)(2,1)}, u32[]{:S(2)}, u32[]{:S(2)}) %collective-permute-start) | collective-permute-done | bytes 524320 | tf_op jit(solution)/shard_map/ppermute | solution.py:15
  84.2 8.1 %collective-permute-start.2 = (bf16[16,64,256]{2,1,0:T(8,128)(2,1)}, bf16[16,64,256]{2,1,0:T(8,128)(2,1)}, u32[]{:S(2)}, u32[]{:S(2)}) collective-permute-start(bf16[16,64,256]{2,1,0:T(8,128)(2,1)} %collective-permute-done), channel_id=1, source_target_pairs={{0,1},{1,2},{2,3},{3,0},{4,5},{5,6},{6,7},{7,4},{8,9},{9,10},{10,1... | collective-permute-start | bytes 1572872 | tf_op jit(solution)/shard_map/ppermute | solution.py:15
  92.3 0.7 reshape.126
  93.0 0.8 copy.54
  93.8 0.7 all_to_all.74
  94.5 0.2 broadcast_in_dim.2
  94.7 1.1 constant_dynamic-update-slice_fusion.3
  95.8 1.1 constant_dynamic-update-slice_fusion.2
  96.9 1.1 constant_dynamic-update-slice_fusion.1
  98.0 5.2 %collective-permute-done.2 = bf16[16,64,256]{2,1,0:T(8,128)(2,1)} collective-permute-done((bf16[16,64,256]{2,1,0:T(8,128)(2,1)}, bf16[16,64,256]{2,1,0:T(8,128)(2,1)}, u32[]{:S(2)}, u32[]{:S(2)}) %collective-permute-start.2) | collective-permute-done | bytes 524320 | tf_op jit(solution)/shard_map/ppermute | solution.py:15
  103.1 1.1 constant_dynamic-update-slice_fusion
  104.2 0.8 convolution_convert_fusion
  105.0 1.0 copy.42
  106.0 1.5 %reshape.127 = bf16[8,2,16384]{2,1,0:T(2,128)(2,1)} reshape(bf16[256,16,64]{2,1,0:T(8,128)(2,1)S(1)} %bitcast.76) | data formatting | bytes 1048576
  107.5 6.1 %all-to-all-start.4 = ((bf16[8,2,16384]{2,1,0:T(2,128)(2,1)}), bf16[8,2,16384]{2,1,0:T(2,128)(2,1)S(1)}, u32[]{:S(2)}, u32[]{:S(2)}) async-start(bf16[8,2,16384]{2,1,0:T(2,128)(2,1)} %reshape.127), calls=%async_computation.4 | async-start | bytes 1048576 | tf_op jit(solution)/shard_map/all_to_all | solution.py:76
  113.6 1.4 %fusion.11 = f32[2048,128]{1,0:T(8,128)} fusion(bf16[2048,128]{1,0:T(8,128)(2,1)S(1)} %fusion.18, bf16[128,128]{1,0:T(8,128)(2,1)S(1)} %copy-done.9), kind=kOutput, calls=%fused_computation.19 | convolution fusion | flops 67895296 | bytes 1605632 | tf_op jit(solution)/shard_map/dot_general | solution.py:41
  115.0 8.3 %all-to-all-done.4 = bf16[8,2,16384]{2,1,0:T(2,128)(2,1)S(1)} async-done(((bf16[8,2,16384]{2,1,0:T(2,128)(2,1)}), bf16[8,2,16384]{2,1,0:T(2,128)(2,1)S(1)}, u32[]{:S(2)}, u32[]{:S(2)}) %all-to-all-start.4) | async-done | bytes 524320 | tf_op jit(solution)/shard_map/all_to_all | solution.py:76
  123.3 0.7 reshape.128
  124.0 0.3 copy.43
  124.3 0.3 convert_bitcast_fusion
  124.5 0.2 copy.44
  124.8 0.2 bitcast_reduce_fusion
  125.0 0.3 multiply_reduce_fusion
  125.5 2.3 %copy.45 = f32[32,64,128]{2,1,0:T(8,128)} copy(f32[32,64,128]{1,0,2:T(8,128)S(1)} %bitcast.71) | data formatting | bytes 2097152 | tf_op jit(solution)/shard_map/convert_element_type | solution.py:77
  127.8 1.9 %fusion.16 = bf16[2048,128]{1,0:T(8,128)(2,1)S(1)} fusion(f32[32,64,128]{2,1,0:T(8,128)} %copy.45, f32[2048]{0:T(1024)S(1)} %rsqrt.33, f32[2048]{0:T(1024)S(1)} %div.38), kind=kLoop, calls=%fused_computation.28 | loop fusion | flops 786432 | bytes 1589248 | tf_op jit(solution)/shard_map/convert_element_type | solution.py:78
  129.8 0.5 fusion.24
  130.3 0.6 multiply_reduce_fusion.1
  131.0 2.1 %fusion.14 = bf16[2048,128]{1,0:T(8,128)(2,1)} fusion(f32[2048,128]{1,0:T(8,128)S(1)} %get-tuple-element.6, bf16[512,128]{1,0:T(8,128)(2,1)S(1)} %copy-done, bf16[128,512]{1,0:T(8,128)(2,1)S(1)} %copy-done.6, f32[2048]{0:T(1024)S(1)} %add_rsqrt_fusion.2, f32[2048]{0:T(1024)S(1)} %broadcast_multiply_fusion.3), kind=kOutput, calls=%fused_computation.22 | convolution fusion | flops 540278784 | bytes 1851392 | tf_op jit(solution)/shard_map/dot_general | solution.py:84
  (32 shorter events, 0.5 us)
Async XLA Ops:
  0.0 130.9 %copy-start = (bf16[512,128]{1,0:T(8,128)(2,1)S(1)}, bf16[512,128]{1,0:T(8,128)(2,1)}, u32[]{:S(2)}) copy-start(bf16[512,128]{1,0:T(8,128)(2,1)} %param.19) | copy-start | bytes 393220
  0.0 5.9 %copy-start.7 = (bf16[128,128]{1,0:T(8,128)(2,1)S(1)}, bf16[128,128]{1,0:T(8,128)(2,1)}, u32[]{:S(2)}) copy-start(bf16[128,128]{1,0:T(8,128)(2,1)} %param.12) | copy-start | bytes 98308
  5.9 0.8 copy-start.3
  7.1 8.3 %copy-start.8 = (bf16[128,128]{1,0:T(8,128)(2,1)S(1)}, bf16[128,128]{1,0:T(8,128)(2,1)}, u32[]{:S(2)}) copy-start(bf16[128,128]{1,0:T(8,128)(2,1)} %param.14) | copy-start | bytes 98308
  10.2 14.9 %all-to-all-start = ((bf16[8,2,16384]{2,1,0:T(2,128)(2,1)}), bf16[8,2,16384]{2,1,0:T(2,128)(2,1)S(1)}, u32[]{:S(2)}, u32[]{:S(2)}) async-start(bf16[8,2,16384]{2,1,0:T(2,128)(2,1)} %reshape.119), calls=%async_computation | async-start | bytes 1048576 | tf_op jit(solution)/shard_map/all_to_all | solution.py:56
  15.4 0.8 copy-start.4
  25.1 13.2 %all-to-all-start.2 = ((bf16[8,2,16384]{2,1,0:T(2,128)(2,1)}), bf16[8,2,16384]{2,1,0:T(2,128)(2,1)S(1)}, u32[]{:S(2)}, u32[]{:S(2)}) async-start(bf16[8,2,16384]{2,1,0:T(2,128)(2,1)} %reshape.123), calls=%async_computation.2 | async-start | bytes 1048576 | tf_op jit(solution)/shard_map/all_to_all | solution.py:63
  38.3 17.0 %all-to-all-start.1 = ((bf16[4,2,32768]{2,1,0:T(2,128)(2,1)}), bf16[4,2,32768]{2,1,0:T(2,128)(2,1)S(1)}, u32[]{:S(2)}, u32[]{:S(2)}) async-start(bf16[4,2,32768]{2,1,0:T(2,128)(2,1)} %reshape.121), calls=%async_computation.1 | async-start | bytes 1048576 | tf_op jit(solution)/shard_map/all_to_all | solution.py:55
  55.3 37.0 %all-to-all-start.3 = ((bf16[4,2,32768]{2,1,0:T(2,128)(2,1)}), bf16[4,2,32768]{2,1,0:T(2,128)(2,1)S(1)}, u32[]{:S(2)}, u32[]{:S(2)}) async-start(bf16[4,2,32768]{2,1,0:T(2,128)(2,1)} %reshape.125), calls=%async_computation.3 | async-start | bytes 1048576 | tf_op jit(solution)/shard_map/all_to_all | solution.py:62
  62.0 22.2 %collective-permute-start = (bf16[16,64,256]{2,1,0:T(8,128)(2,1)}, bf16[16,64,256]{2,1,0:T(8,128)(2,1)}, u32[]{:S(2)}, u32[]{:S(2)}) collective-permute-start(bf16[16,64,256]{2,1,0:T(8,128)(2,1)} %all_to_all.66), channel_id=1, source_target_pairs={{0,1},{1,2},{2,3},{3,0},{4,5},{5,6},{6,7},{7,4},{8,9},{9,10},{10,1... | collective-permute-start | bytes 1572872 | tf_op jit(solution)/shard_map/ppermute | solution.py:15
  63.8 33.1 %collective-permute-start.1 = (bf16[16,64,256]{2,1,0:T(8,128)(2,1)}, bf16[16,64,256]{2,1,0:T(8,128)(2,1)}, u32[]{:S(2)}, u32[]{:S(2)}) collective-permute-start(bf16[16,64,256]{2,1,0:T(8,128)(2,1)} %all_to_all.66), channel_id=1, source_target_pairs={{0,3},{1,0},{2,1},{3,2},{4,7},{5,4},{6,5},{7,6},{8,11},{9,8},{10,9... | collective-permute-start | bytes 1572872 | tf_op jit(solution)/shard_map/ppermute | solution.py:18
  84.2 18.9 %collective-permute-start.2 = (bf16[16,64,256]{2,1,0:T(8,128)(2,1)}, bf16[16,64,256]{2,1,0:T(8,128)(2,1)}, u32[]{:S(2)}, u32[]{:S(2)}) collective-permute-start(bf16[16,64,256]{2,1,0:T(8,128)(2,1)} %collective-permute-done), channel_id=1, source_target_pairs={{0,1},{1,2},{2,3},{3,0},{4,5},{5,6},{6,7},{7,4},{8,9},{9,10},{10,1... | collective-permute-start | bytes 1572872 | tf_op jit(solution)/shard_map/ppermute | solution.py:15
  105.0 8.6 %copy-start.9 = (bf16[128,128]{1,0:T(8,128)(2,1)S(1)}, bf16[128,128]{1,0:T(8,128)(2,1)}, u32[]{:S(2)}) copy-start(bf16[128,128]{1,0:T(8,128)(2,1)} %param.16) | copy-start | bytes 98308
  107.5 15.9 %all-to-all-start.4 = ((bf16[8,2,16384]{2,1,0:T(2,128)(2,1)}), bf16[8,2,16384]{2,1,0:T(2,128)(2,1)S(1)}, u32[]{:S(2)}, u32[]{:S(2)}) async-start(bf16[8,2,16384]{2,1,0:T(2,128)(2,1)} %reshape.127), calls=%async_computation.4 | async-start | bytes 1048576 | tf_op jit(solution)/shard_map/all_to_all | solution.py:76
  125.5 4.3 %copy-start.1 = (bf16[32,64,128]{2,1,0:T(8,128)(2,1)S(1)}, bf16[32,64,128]{2,1,0:T(8,128)(2,1)}, u32[]{:S(2)}) copy-start(bf16[32,64,128]{2,1,0:T(8,128)(2,1)} %param.10) | copy-start | bytes 1572868
  125.5 4.3 %copy-start.5 = (bf16[128,128]{1,0:T(8,128)(2,1)S(1)}, bf16[128,128]{1,0:T(8,128)(2,1)}, u32[]{:S(2)}) copy-start(bf16[128,128]{1,0:T(8,128)(2,1)} %param.17) | copy-start | bytes 98308
  127.8 1.9 %copy-start.2 = (f32[2048,128]{1,0:T(8,128)S(1)}, f32[2048,128]{1,0:T(8,128)}, u32[]{:S(2)}) copy-start(f32[2048,128]{1,0:T(8,128)} %fusion.11) | copy-start | bytes 3145732
  129.8 1.2 copy-start.6
